TPU v7x, 128 devices: a whole 4x4x4 slice. The times are simulated.
128 devices in a mesh: gx: 16 (over z, x), gy: 8 (over y, core).
Axes of the slice: x: 4, y: 4, z: 4, core: 2. Of those that a mesh axis runs over, the one named last changes fastest.
Arguments:
- tokens: bfloat16 [2048, 8192], P('gy', 'gx'), may hold values from -6 to 6
- gate_base_weight: bfloat16 [8192, 29568], P('gx', 'gy'), may hold values from -0.0625 to 0.0625
- up_base_weight: bfloat16 [8192, 29568], P('gx', 'gy'), may hold values from -0.0625 to 0.0625
- adapter_down_maps: bfloat16 [128, 8192, 128], P(('gx', 'gy')), may hold values from -0.0625 to 0.0625
- adapter_up_maps: bfloat16 [128, 128, 29568], P(('gx', 'gy')), may hold values from -0.75 to 0.75
- tenant: int32 [2048, 1], replicated, may hold values from 0 to 127; in each aligned block of 128 rows (0 to 127, 128 to 255, ...) at most 4 rows name the same one
- tenant_slot_index: int32 [128], replicated, may hold values from 0 to 127, as said below
Outputs:
- hidden: bfloat16 [2048, 29568], P('gx', 'gy')
Inputs may be any that keep to these rules, and one draw needn't show every extreme that they name: In each aligned block of 128 rows no tenant names more than 4 rows, and in some block a tenant names exactly 4. `tenant_slot_index`: A permutation of the slots; slot s is held by device s of gx+gy, gx the slower index.
All inputs are finite; a program needn't handle non-finite values.
Results may differ from a plain program's by a relative error of at most 0.019.
Values may be sent and summed in bfloat16 or wider, within the bound.
No kernel may reach another device: no remote copies, remote signals or barrier semaphores. Data moves between devices by JAX's collectives and lax.ppermute only.
A program may use at most 192 MiB of HBM per device.

v0:
```python
import jax
import jax.numpy as jnp
from jax import lax
from jax.sharding import PartitionSpec as P
from jax.experimental.layout import Layout, with_layout_constraint

CAP = 4


def body(
    tokens,
    gate_base_weight,
    up_base_weight,
    adapter_down_maps,
    adapter_up_maps,
    tenant,
    tenant_slot_index,
):
    tile_grid_rows = lax.axis_size("gx")
    tile_grid_columns = lax.axis_size("gy")
    devices = tile_grid_rows * tile_grid_columns
    row_gx = lax.axis_index("gx")
    row_gy = lax.axis_index("gy")
    local_rows = tokens.shape[0]
    tile_width = tokens.shape[1]
    total_rows = tenant.shape[0]
    block = total_rows // tile_grid_rows
    groups = local_rows // block
    tenants = tenant_slot_index.shape[0]
    column_count = gate_base_weight.shape[1]
    doubled_rank = adapter_down_maps.shape[2]
    adapter_rank_width = doubled_rank // 2
    owner_rows = tile_grid_rows * CAP

    slot_all = jnp.sum(
        jnp.where(tenant == lax.iota(jnp.int32, tenants)[None, :], tenant_slot_index[None, :], 0),
        axis=1,
    )
    by_block = slot_all.reshape(tile_grid_rows, block)
    earlier = lax.iota(jnp.int32, block)[None, :] < lax.iota(jnp.int32, block)[:, None]
    same = (by_block[:, :, None] == by_block[:, None, :]) & earlier[None, :, :]
    position = jnp.sum(same.astype(jnp.int32), axis=2).reshape(total_rows)

    send_slot = lax.dynamic_slice_in_dim(slot_all, row_gy * local_rows, local_rows)
    send_rank = lax.dynamic_slice_in_dim(position, row_gy * local_rows, local_rows)
    target = (send_slot * groups + lax.iota(jnp.int32, local_rows) // block) * CAP + send_rank
    chosen = (target[None, :] == lax.iota(jnp.int32, devices * groups * CAP)[:, None]).astype(jnp.bfloat16)
    outgoing = jnp.dot(chosen, tokens, preferred_element_type=jnp.float32).astype(jnp.bfloat16)
    arrived = lax.all_to_all(
        outgoing.reshape(devices, groups * CAP, tile_width),
        ("gx", "gy"),
        split_axis=0,
        concat_axis=0,
        tiled=True,
    )
    arrived = arrived.reshape(tile_grid_rows, tile_grid_columns * groups * CAP, tile_width)
    down_local = adapter_down_maps[0].reshape(tile_grid_rows, tile_width, doubled_rank)
    low = jnp.einsum("isk,ikr->sr", arrived, down_local, preferred_element_type=jnp.float32).astype(
        jnp.bfloat16
    )

    gate_up_map = adapter_up_maps[0, :adapter_rank_width].reshape(
        adapter_rank_width, tile_grid_columns, column_count
    )
    up_up_map = adapter_up_maps[0, adapter_rank_width:].reshape(
        adapter_rank_width, tile_grid_columns, column_count
    )
    delta_gate = jnp.einsum(
        "qr,rjf->jqf", low[:, :adapter_rank_width], gate_up_map, preferred_element_type=jnp.float32
    ).astype(jnp.bfloat16)
    delta_up = jnp.einsum(
        "qr,rjf->jqf", low[:, adapter_rank_width:], up_up_map, preferred_element_type=jnp.float32
    ).astype(jnp.bfloat16)
    got_gate = lax.all_to_all(delta_gate, "gy", split_axis=0, concat_axis=0, tiled=True)
    got_up = lax.all_to_all(delta_up, "gy", split_axis=0, concat_axis=0, tiled=True)
    got_gate = got_gate.reshape(tile_grid_columns * owner_rows, column_count)
    got_up = got_up.reshape(tile_grid_columns * owner_rows, column_count)

    entries = tile_grid_columns * owner_rows
    mine = slot_all // tile_grid_columns == row_gx
    entry = (slot_all % tile_grid_columns) * owner_rows + (lax.iota(jnp.int32, total_rows) // block) * CAP + position
    entry = jnp.where(mine, entry, entries)
    row_of_entry = jnp.zeros((entries,), jnp.int32).at[entry].set(
        lax.iota(jnp.int32, total_rows), mode="drop"
    )

    gathered = lax.all_gather(tokens, "gy", axis=0, tiled=True)
    row_major = Layout(major_to_minor=(0, 1))
    gate_part = with_layout_constraint(
        jnp.dot(gathered, gate_base_weight, preferred_element_type=jnp.float32).astype(jnp.bfloat16),
        row_major,
    )
    gate_part = gate_part.at[row_of_entry].add(got_gate)
    gate_sum = lax.psum_scatter(gate_part, "gx", scatter_dimension=0, tiled=True).astype(jnp.float32)
    up_part = with_layout_constraint(
        jnp.dot(gathered, up_base_weight, preferred_element_type=jnp.float32).astype(jnp.bfloat16),
        row_major,
    )
    up_part = up_part.at[row_of_entry].add(got_up)
    up_sum = lax.psum_scatter(up_part, "gx", scatter_dimension=0, tiled=True).astype(jnp.float32)
    return (jax.nn.silu(gate_sum) * up_sum).astype(jnp.bfloat16)


def solution(mesh):
    return jax.shard_map(
        body,
        mesh=mesh,
        in_specs=(
            P("gy", "gx"),
            P("gx", "gy"),
            P("gx", "gy"),
            P(("gx", "gy"), None, None),
            P(("gx", "gy"), None, None),
            P(),
            P(),
        ),
        out_specs=P("gx", "gy"),
        check_vma=False,
    )
```

profile of v0, /device:TPU:1, one launch (start us, length us, event | category | flops | bytes accessed | tf_op | source)
XLA Modules:
  0.0 342.3 jit_solution(3717130775793756142)
XLA Ops:
  6.5 0.0 copy-start
  6.5 0.0 all-gather.2.cloned.1.call-start
  6.5 0.7 all-gather.2.cloned.1.call-update
  7.3 1.3 select_reduce_fusion
  8.6 0.6 convert_reduce_fusion
  9.3 0.1 fusion.18
  9.4 2.4 fusion.9
  11.8 11.5 %all-to-all-start = ((bf16[128,8,512]{2,1,0:T(8,128)(2,1)}), bf16[128,8,512]{2,1,0:T(8,128)(2,1)S(1)}, u32[]{:S(2)}, u32[]{:S(2)}) async-start(bf16[128,8,512]{2,1,0:T(8,128)(2,1)} %fusion.9), calls=%async_computation | async-start | bytes 2097152 | tf_op jit(solution)/shard_map/all_to_all | solution.py:49
  23.3 5.4 %fusion.21 = (bf16[1,64,29568]{2,1,0:T(8,128)(2,1)}, bf16[1,64,29568]{2,1,0:T(8,128)(2,1)}) fusion(bf16[1,128,29568]{2,1,0:T(8,128)(2,1)} %param.11), kind=kLoop, calls=%fused_computation.55 | loop fusion | bytes 15138816 | tf_op jit(solution)/shard_map/slice | solution.py:62
  28.7 7.5 %reshape_squeeze.11 = bf16[64,8,3696]{2,1,0:T(8,128)(2,1)} reshape(bf16[1,64,29568]{2,1,0:T(8,128)(2,1)} %get-tuple-element.6) | data formatting | bytes 7569408 | tf_op jit(solution)/shard_map/reshape;squeeze | solution.py:65
  36.2 7.3 %all-to-all-done = bf16[128,8,512]{2,1,0:T(8,128)(2,1)S(1)} async-done(((bf16[128,8,512]{2,1,0:T(8,128)(2,1)}), bf16[128,8,512]{2,1,0:T(8,128)(2,1)S(1)}, u32[]{:S(2)}, u32[]{:S(2)}) %all-to-all-start) | async-done | bytes 1048608 | tf_op jit(solution)/shard_map/all_to_all | solution.py:49
  43.5 0.0 copy-done
  43.5 0.5 fusion.10
  44.1 5.2 %fusion.1 = bf16[8,64,3696]{2,1,0:T(8,128)(2,1)} fusion(bf16[64,8,3696]{2,1,0:T(8,128)(2,1)} %reshape_squeeze.11, bf16[64,128]{1,0:T(8,128)(2,1)S(1)} %fusion.10), kind=kOutput, calls=%fused_computation.8 | convolution fusion | flops 244113408 | bytes 7585792 | tf_op jit(solution)/shard_map/qr,rjf->jqf/dot_general | solution.py:71
  49.3 4.5 %all-to-all-start.2 = ((bf16[8,64,3696]{2,1,0:T(8,128)(2,1)}), bf16[8,64,3696]{2,1,0:T(8,128)(2,1)}, u32[]{:S(2)}, u32[]{:S(2)}) async-start(bf16[8,64,3696]{2,1,0:T(8,128)(2,1)} %fusion.1), calls=%async_computation.3 | async-start | bytes 7602176 | tf_op jit(solution)/shard_map/all_to_all | solution.py:75
  53.8 0.0 reduce-scatter.5.cloned.1.call-start
  53.8 0.1 compare_select_fusion
  53.9 8.5 %scatter_custom_fusion = s32[512]{0:T(512)S(1)} fusion(s32[2048]{0:T(1024)S(1)} %bitcast.40, s32[2048]{0:T(1024)S(1)} %iota.32, s32[]{:T(128)} %constant.64.clone.1), kind=kCustom, calls=%fused_computation.53 | custom fusion | bytes 2052 | tf_op jit(solution)/shard_map/scatter | solution.py:83
  62.5 0.0 all-gather.2.cloned.1.call-done
  62.5 14.0 %convolution_convert_fusion = bf16[2048,3696]{1,0:T(8,128)(2,1)} fusion(bf16[2048,512]{1,0:T(8,128)(2,1)} %all-gather.2.cloned.1.call-done, bf16[512,3696]{0,1:T(8,128)(2,1)} %param.9), kind=kOutput, calls=%fused_computation.3 | convolution fusion | flops 7758643200 | bytes 21020672 | tf_op jit(solution)/shard_map/dot_general | solution.py:96
  76.5 21.9 %all-to-all-done.2 = bf16[8,64,3696]{2,1,0:T(8,128)(2,1)} async-done(((bf16[8,64,3696]{2,1,0:T(8,128)(2,1)}), bf16[8,64,3696]{2,1,0:T(8,128)(2,1)}, u32[]{:S(2)}, u32[]{:S(2)}) %all-to-all-start.2) | async-done | bytes 3784736 | tf_op jit(solution)/shard_map/all_to_all | solution.py:75
  98.4 26.9 %scatter_fusion.1 = bf16[2048,3696]{1,0:T(8,128)(2,1)} fusion(bf16[2048,3696]{1,0:T(8,128)(2,1)} %convolution_convert_fusion, s32[512]{0:T(512)S(1)} %compare_select_fusion.5, bf16[512,3696]{1,0:T(8,128)(2,1)} %bitcast.15), kind=kCustom, calls=%fused_computation.2 | custom fusion | flops 1892352 | bytes 11356160 | tf_op jit(solution)/shard_map/scatter-add | solution.py:99
  125.3 0.0 reduce-scatter.5.cloned.1.call-update
  125.3 7.5 %reshape_squeeze.10 = bf16[64,8,3696]{2,1,0:T(8,128)(2,1)} reshape(bf16[1,64,29568]{2,1,0:T(8,128)(2,1)} %get-tuple-element.5) | data formatting | bytes 7569408 | tf_op jit(solution)/shard_map/reshape;squeeze | solution.py:62
  132.9 5.3 %fusion = bf16[8,64,3696]{2,1,0:T(8,128)(2,1)} fusion(bf16[64,8,3696]{2,1,0:T(8,128)(2,1)} %reshape_squeeze.10, bf16[64,128]{1,0:T(8,128)(2,1)S(1)} %fusion.10), kind=kOutput, calls=%fused_computation.7 | convolution fusion | flops 244113408 | bytes 7585792 | tf_op jit(solution)/shard_map/qr,rjf->jqf/dot_general | solution.py:68
  138.2 0.0 copy-start.2
  138.2 5.3 %all-to-all-start.1 = ((bf16[8,64,3696]{2,1,0:T(8,128)(2,1)}), bf16[8,64,3696]{2,1,0:T(8,128)(2,1)}, u32[]{:S(2)}, u32[]{:S(2)}) async-start(bf16[8,64,3696]{2,1,0:T(8,128)(2,1)} %fusion), calls=%async_computation.1 | async-start | bytes 7602176 | tf_op jit(solution)/shard_map/all_to_all | solution.py:74
  143.5 0.0 reduce-scatter.3.cloned.1.call-start
  143.5 0.0 copy-done.2
  143.5 13.3 %convolution_convert_fusion.1 = bf16[2048,3696]{1,0:T(8,128)(2,1)} fusion(bf16[2048,512]{1,0:T(8,128)(2,1)S(1)} %copy-done.2, bf16[512,3696]{0,1:T(8,128)(2,1)} %param.8), kind=kOutput, calls=%fused_computation.4 | convolution fusion | flops 7758643200 | bytes 21020672 | tf_op jit(solution)/shard_map/dot_general | solution.py:90
  156.8 31.4 %all-to-all-done.1 = bf16[8,64,3696]{2,1,0:T(8,128)(2,1)} async-done(((bf16[8,64,3696]{2,1,0:T(8,128)(2,1)}), bf16[8,64,3696]{2,1,0:T(8,128)(2,1)}, u32[]{:S(2)}, u32[]{:S(2)}) %all-to-all-start.1) | async-done | bytes 3784736 | tf_op jit(solution)/shard_map/all_to_all | solution.py:74
  188.2 27.0 %scatter_fusion = bf16[2048,3696]{1,0:T(8,128)(2,1)} fusion(bf16[2048,3696]{1,0:T(8,128)(2,1)} %convolution_convert_fusion.1, s32[512]{0:T(512)S(1)} %compare_select_fusion.5, bf16[512,3696]{1,0:T(8,128)(2,1)} %bitcast.12), kind=kCustom, calls=%fused_computation.1 | custom fusion | flops 1892352 | bytes 11356160 | tf_op jit(solution)/shard_map/scatter-add | solution.py:93
  215.2 0.0 reduce-scatter.3.cloned.1.call-update
  215.2 0.0 copy-start.1
  215.2 11.0 %reduce-scatter.5.cloned.1.call-done = bf16[128,3696]{1,0:T(8,128)(2,1)} async-done(((bf16[2048,3696]{1,0:T(8,128)(2,1)}), bf16[128,3696]{1,0:T(8,128)(2,1)}) %reduce-scatter.5.cloned.1.call-update) | async-done | bytes 946192 | tf_op jit(solution)/shard_map/reduce_scatter | solution.py:100
  226.2 105.9 %reduce-scatter.3.cloned.1.call-done = bf16[128,3696]{1,0:T(8,128)(2,1)} async-done(((bf16[2048,3696]{1,0:T(8,128)(2,1)}), bf16[128,3696]{1,0:T(8,128)(2,1)}) %reduce-scatter.3.cloned.1.call-update) | async-done | bytes 946192 | tf_op jit(solution)/shard_map/reduce_scatter | solution.py:94
  332.2 2.0 fusion.8
  334.2 1.3 copy.14
  335.5 0.0 copy-done.1
  (3 shorter events, 0.0 us)
Async XLA Ops:
  6.5 37.0 %copy-start = (bf16[1,8192,128]{2,1,0:T(8,128)(2,1)S(1)}, bf16[1,8192,128]{2,1,0:T(8,128)(2,1)}, u32[]{:S(2)}) copy-start(bf16[1,8192,128]{2,1,0:T(8,128)(2,1)} %param.10) | copy-start | bytes 6291460
  6.5 55.9 %all-gather.2.cloned.1.call-start = ((), (), s32[]{:S(2)}) async-start(), calls=%async_computation.5 | async-start | bytes 2359296 | tf_op jit(solution)/shard_map/all_gather | solution.py:87
  11.8 31.8 %all-to-all-start = ((bf16[128,8,512]{2,1,0:T(8,128)(2,1)}), bf16[128,8,512]{2,1,0:T(8,128)(2,1)S(1)}, u32[]{:S(2)}, u32[]{:S(2)}) async-start(bf16[128,8,512]{2,1,0:T(8,128)(2,1)} %fusion.9), calls=%async_computation | async-start | bytes 2097152 | tf_op jit(solution)/shard_map/all_to_all | solution.py:49
  49.3 49.1 %all-to-all-start.2 = ((bf16[8,64,3696]{2,1,0:T(8,128)(2,1)}), bf16[8,64,3696]{2,1,0:T(8,128)(2,1)}, u32[]{:S(2)}, u32[]{:S(2)}) async-start(bf16[8,64,3696]{2,1,0:T(8,128)(2,1)} %fusion.1), calls=%async_computation.3 | async-start | bytes 7602176 | tf_op jit(solution)/shard_map/all_to_all | solution.py:75
  53.8 172.4 %reduce-scatter.5.cloned.1.call-start = ((), (), s32[]{:S(2)}) async-start(), calls=%async_computation.7 | async-start | bytes 16154624 | tf_op jit(solution)/shard_map/reduce_scatter | solution.py:100
  138.2 5.3 %copy-start.2 = (bf16[2048,512]{1,0:T(8,128)(2,1)S(1)}, bf16[2048,512]{1,0:T(8,128)(2,1)}, u32[]{:S(2)}) copy-start(bf16[2048,512]{1,0:T(8,128)(2,1)} %all-gather.2.cloned.1.call-done) | copy-start | bytes 6291460
  138.2 50.0 %all-to-all-start.1 = ((bf16[8,64,3696]{2,1,0:T(8,128)(2,1)}), bf16[8,64,3696]{2,1,0:T(8,128)(2,1)}, u32[]{:S(2)}, u32[]{:S(2)}) async-start(bf16[8,64,3696]{2,1,0:T(8,128)(2,1)} %fusion), calls=%async_computation.1 | async-start | bytes 7602176 | tf_op jit(solution)/shard_map/all_to_all | solution.py:74
  143.5 188.7 %reduce-scatter.3.cloned.1.call-start = ((), (), s32[]{:S(2)}) async-start(), calls=%async_computation.6 | async-start | bytes 16154624 | tf_op jit(solution)/shard_map/reduce_scatter | solution.py:94
  215.2 120.4 %copy-start.1 = (bf16[1,8192,128]{2,1,0:T(8,128)(2,1)S(1)}, bf16[1,8192,128]{2,1,0:T(8,128)(2,1)}, u32[]{:S(2)}) copy-start(bf16[1,8192,128]{2,1,0:T(8,128)(2,1)} %param.10) | copy-start | bytes 6291460
Sparse Core Ops, SparseCore 0:
  9.1 39.2 all-gather.1
  125.5 100.7 reduce-scatter.4
  230.1 102.0 reduce-scatter.2
where the time goes:
time: 348 us; the launch traced here: 342 us
  waiting for transfers between devices  178 us (51%)
  other arithmetic  58.1 us (17%)
  matrix products  40.8 us (12%)
  local copies, waits for them, and re-layouts  30.3 us (9%)
  starting transfers between devices  21.3 us (6%)
  between operations  13.4 us (4%)
    reduce_scatter x1, waiting for transfers between devices, body(): lax.psum_scatter(gate_part, 'gx', scatter_dimension=0, tiled=True)  106 us
    all_to_all x1, waiting for transfers between devices, body(): lax.all_to_all(delta_gate, 'gy', split_axis=0, concat_axis=0, tiled=True)  31.4 us
    scatter-add x1, other arithmetic, body(): gate_part = gate_part.at[row_of_entry].add(got_gate)  27 us
    scatter-add x1, other arithmetic, body(): up_part = up_part.at[row_of_entry].add(got_up)  26.9 us
    all_to_all x1, waiting for transfers between devices, body(): lax.all_to_all(delta_up, 'gy', split_axis=0, concat_axis=0, tiled=True)  21.9 us
    dot_general x1, matrix products, body(): jnp.dot(gathered, up_base_weight, preferred_element_type=jnp.float32)  14 us
    dot_general x1, matrix products, body(): jnp.dot(gathered, gate_base_weight, preferred_element_type=jnp.float32)  13.3 us
    all_to_all x1, starting transfers between devices, body(): lax.all_to_all(outgoing.reshape(devices, groups * CAP, tile_width), ('gx'...  11.5 us
  transfers between devices with their start and end apart: 6, of which 5 were waited for; matrix products, arithmetic and copies ran while one was open for 29% of the time, Pallas kernels for 0%

commit v1 on v0

--- a/solution.py
+++ b/solution.py
@@ -32,10 +32,7 @@
     adapter_rank_width = doubled_rank // 2
     owner_rows = tile_grid_rows * CAP
 
-    slot_all = jnp.sum(
-        jnp.where(tenant == lax.iota(jnp.int32, tenants)[None, :], tenant_slot_index[None, :], 0),
-        axis=1,
-    )
+    slot_all = jnp.take(tenant_slot_index, tenant[:, 0], axis=0, mode="clip")
     by_block = slot_all.reshape(tile_grid_rows, block)
     earlier = lax.iota(jnp.int32, block)[None, :] < lax.iota(jnp.int32, block)[:, None]
     same = (by_block[:, :, None] == by_block[:, None, :]) & earlier[None, :, :]

time: 348 us -> 357 us (1.026)
  local copies, waits for them, and re-layouts: 30.3 us -> 43.1 us
    gather x0 -> x1, local copies, waits for them, and re-layouts: none -> 12.6 us  [body(): slot_all = jnp.take(tenant_slot_index, tenant[:, 0], axis=0, mode='clip')]
  transfers between devices with their start and end apart: 6 -> 6, of which waited for: 5 -> 5; matrix products, arithmetic and copies ran while one was open for 29% -> 31% of each run, Pallas kernels for 0% -> 0%
where the time goes in v1:
time: 357 us; the launch traced here: 351 us
  waiting for transfers between devices  175 us (49%)
  other arithmetic  57.3 us (16%)
  local copies, waits for them, and re-layouts  43.1 us (12%)
  matrix products  39.7 us (11%)
  starting transfers between devices  22.6 us (6%)
  between operations  13.4 us (4%)
    reduce_scatter x1, waiting for transfers between devices, body(): lax.psum_scatter(gate_part, 'gx', scatter_dimension=0, tiled=True)  106 us
    all_to_all x1, waiting for transfers between devices, body(): lax.all_to_all(delta_gate, 'gy', split_axis=0, concat_axis=0, tiled=True)  31.4 us
    scatter-add x1, other arithmetic, body(): up_part = up_part.at[row_of_entry].add(got_up)  26.9 us
    scatter-add x1, other arithmetic, body(): gate_part = gate_part.at[row_of_entry].add(got_gate)  26.8 us
    all_to_all x1, waiting for transfers between devices, body(): lax.all_to_all(delta_up, 'gy', split_axis=0, concat_axis=0, tiled=True)  22 us
    dot_general x1, matrix products, body(): jnp.dot(gathered, up_base_weight, preferred_element_type=jnp.float32)  14 us
    dot_general x1, matrix products, body(): jnp.dot(gathered, gate_base_weight, preferred_element_type=jnp.float32)  13.3 us
    gather x1, local copies, waits for them, and re-layouts, body(): slot_all = jnp.take(tenant_slot_index, tenant[:, 0], axis=0, mode='clip')  12.6 us
  transfers between devices with their start and end apart: 6, of which 5 were waited for; matrix products, arithmetic and copies ran while one was open for 31% of the time, Pallas kernels for 0%

profile of v1, /device:TPU:1, one launch (start us, length us, event | category | flops | bytes accessed | tf_op | source)
XLA Modules:
  0.0 350.8 jit_solution(11032536235612824819)
XLA Ops:
  6.5 0.0 copy-start
  6.5 0.0 copy-start.2
  6.5 0.0 all-gather.2.cloned.1.call-start
  6.5 0.7 all-gather.2.cloned.1.call-update
  7.3 0.7 broadcast_clamp_fusion
  8.0 0.0 copy-done.2
  8.0 0.0 copy-start.3
  8.0 12.6 %gather_fusion = s32[2048]{0:T(1024)S(1)} fusion(s32[128]{0:T(128)S(1)} %copy-done.2, s32[2048]{0:T(1024)S(1)} %broadcast_clamp_fusion), kind=kCustom, calls=%fused_computation | custom fusion | bytes 24576 | tf_op jit(solution)/shard_map/jit(_take)/gather | solution.py:35
  20.6 0.6 convert_reduce_fusion
  21.3 0.1 fusion.18
  21.3 0.0 copy-done.3
  21.3 1.5 fusion.9
  22.8 11.5 %all-to-all-start = ((bf16[128,8,512]{2,1,0:T(8,128)(2,1)}), bf16[128,8,512]{2,1,0:T(8,128)(2,1)S(1)}, u32[]{:S(2)}, u32[]{:S(2)}) async-start(bf16[128,8,512]{2,1,0:T(8,128)(2,1)} %fusion.9), calls=%async_computation | async-start | bytes 2097152 | tf_op jit(solution)/shard_map/all_to_all | solution.py:46
  34.3 5.5 %fusion.21 = (bf16[1,64,29568]{2,1,0:T(8,128)(2,1)}, bf16[1,64,29568]{2,1,0:T(8,128)(2,1)}) fusion(bf16[1,128,29568]{2,1,0:T(8,128)(2,1)} %param.11), kind=kLoop, calls=%fused_computation.55 | loop fusion | bytes 15138816 | tf_op jit(solution)/shard_map/slice | solution.py:59
  39.8 7.5 %reshape_squeeze.11 = bf16[64,8,3696]{2,1,0:T(8,128)(2,1)} reshape(bf16[1,64,29568]{2,1,0:T(8,128)(2,1)} %get-tuple-element.6) | data formatting | bytes 7569408 | tf_op jit(solution)/shard_map/reshape;squeeze | solution.py:62
  47.3 5.9 %all-to-all-done = bf16[128,8,512]{2,1,0:T(8,128)(2,1)S(1)} async-done(((bf16[128,8,512]{2,1,0:T(8,128)(2,1)}), bf16[128,8,512]{2,1,0:T(8,128)(2,1)S(1)}, u32[]{:S(2)}, u32[]{:S(2)}) %all-to-all-start) | async-done | bytes 1048608 | tf_op jit(solution)/shard_map/all_to_all | solution.py:46
  53.3 0.0 copy-done
  53.3 0.5 fusion.10
  53.8 5.2 %fusion.1 = bf16[8,64,3696]{2,1,0:T(8,128)(2,1)} fusion(bf16[64,8,3696]{2,1,0:T(8,128)(2,1)} %reshape_squeeze.11, bf16[64,128]{1,0:T(8,128)(2,1)S(1)} %fusion.10), kind=kOutput, calls=%fused_computation.9 | convolution fusion | flops 244113408 | bytes 7585792 | tf_op jit(solution)/shard_map/qr,rjf->jqf/dot_general | solution.py:68
  59.0 5.7 %all-to-all-start.2 = ((bf16[8,64,3696]{2,1,0:T(8,128)(2,1)}), bf16[8,64,3696]{2,1,0:T(8,128)(2,1)}, u32[]{:S(2)}, u32[]{:S(2)}) async-start(bf16[8,64,3696]{2,1,0:T(8,128)(2,1)} %fusion.1), calls=%async_computation.3 | async-start | bytes 7602176 | tf_op jit(solution)/shard_map/all_to_all | solution.py:72
  64.6 0.0 reduce-scatter.5.cloned.1.call-start
  64.6 0.1 compare_select_fusion
  64.7 8.5 %scatter_custom_fusion = s32[512]{0:T(512)S(1)} fusion(s32[2048]{0:T(1024)S(1)} %bitcast.40, s32[2048]{0:T(1024)S(1)} %iota.30, s32[]{:T(128)} %constant.64.clone.1), kind=kCustom, calls=%fused_computation.53 | custom fusion | bytes 2052 | tf_op jit(solution)/shard_map/scatter | solution.py:80
  73.2 0.0 all-gather.2.cloned.1.call-done
  73.3 14.0 %convolution_convert_fusion = bf16[2048,3696]{1,0:T(8,128)(2,1)} fusion(bf16[2048,512]{1,0:T(8,128)(2,1)} %all-gather.2.cloned.1.call-done, bf16[512,3696]{0,1:T(8,128)(2,1)} %param.9), kind=kOutput, calls=%fused_computation.4 | convolution fusion | flops 7758643200 | bytes 21020672 | tf_op jit(solution)/shard_map/dot_general | solution.py:93
  87.3 22.0 %all-to-all-done.2 = bf16[8,64,3696]{2,1,0:T(8,128)(2,1)} async-done(((bf16[8,64,3696]{2,1,0:T(8,128)(2,1)}), bf16[8,64,3696]{2,1,0:T(8,128)(2,1)}, u32[]{:S(2)}, u32[]{:S(2)}) %all-to-all-start.2) | async-done | bytes 3784736 | tf_op jit(solution)/shard_map/all_to_all | solution.py:72
  109.3 26.9 %scatter_fusion.1 = bf16[2048,3696]{1,0:T(8,128)(2,1)} fusion(bf16[2048,3696]{1,0:T(8,128)(2,1)} %convolution_convert_fusion, s32[512]{0:T(512)S(1)} %compare_select_fusion.5, bf16[512,3696]{1,0:T(8,128)(2,1)} %bitcast.15), kind=kCustom, calls=%fused_computation.3 | custom fusion | flops 1892352 | bytes 11356160 | tf_op jit(solution)/shard_map/scatter-add | solution.py:96
  136.3 0.0 reduce-scatter.5.cloned.1.call-update
  136.3 7.6 %reshape_squeeze.10 = bf16[64,8,3696]{2,1,0:T(8,128)(2,1)} reshape(bf16[1,64,29568]{2,1,0:T(8,128)(2,1)} %get-tuple-element.5) | data formatting | bytes 7569408 | tf_op jit(solution)/shard_map/reshape;squeeze | solution.py:59
  143.9 5.2 %fusion = bf16[8,64,3696]{2,1,0:T(8,128)(2,1)} fusion(bf16[64,8,3696]{2,1,0:T(8,128)(2,1)} %reshape_squeeze.10, bf16[64,128]{1,0:T(8,128)(2,1)S(1)} %fusion.10), kind=kOutput, calls=%fused_computation.8 | convolution fusion | flops 244113408 | bytes 7585792 | tf_op jit(solution)/shard_map/qr,rjf->jqf/dot_general | solution.py:65
  149.1 0.0 copy-start.4
  149.1 5.4 %all-to-all-start.1 = ((bf16[8,64,3696]{2,1,0:T(8,128)(2,1)}), bf16[8,64,3696]{2,1,0:T(8,128)(2,1)}, u32[]{:S(2)}, u32[]{:S(2)}) async-start(bf16[8,64,3696]{2,1,0:T(8,128)(2,1)} %fusion), calls=%async_computation.1 | async-start | bytes 7602176 | tf_op jit(solution)/shard_map/all_to_all | solution.py:71
  154.6 0.0 reduce-scatter.3.cloned.1.call-start
  154.6 0.0 copy-done.4
  154.6 13.3 %convolution_convert_fusion.1 = bf16[2048,3696]{1,0:T(8,128)(2,1)} fusion(bf16[2048,512]{1,0:T(8,128)(2,1)S(1)} %copy-done.4, bf16[512,3696]{0,1:T(8,128)(2,1)} %param.8), kind=kOutput, calls=%fused_computation.5 | convolution fusion | flops 7758643200 | bytes 21020672 | tf_op jit(solution)/shard_map/dot_general | solution.py:87
  167.8 31.4 %all-to-all-done.1 = bf16[8,64,3696]{2,1,0:T(8,128)(2,1)} async-done(((bf16[8,64,3696]{2,1,0:T(8,128)(2,1)}), bf16[8,64,3696]{2,1,0:T(8,128)(2,1)}, u32[]{:S(2)}, u32[]{:S(2)}) %all-to-all-start.1) | async-done | bytes 3784736 | tf_op jit(solution)/shard_map/all_to_all | solution.py:71
  199.3 26.8 %scatter_fusion = bf16[2048,3696]{1,0:T(8,128)(2,1)} fusion(bf16[2048,3696]{1,0:T(8,128)(2,1)} %convolution_convert_fusion.1, s32[512]{0:T(512)S(1)} %compare_select_fusion.5, bf16[512,3696]{1,0:T(8,128)(2,1)} %bitcast.12), kind=kCustom, calls=%fused_computation.2 | custom fusion | flops 1892352 | bytes 11356160 | tf_op jit(solution)/shard_map/scatter-add | solution.py:90
  226.1 0.0 reduce-scatter.3.cloned.1.call-update
  226.1 0.0 copy-start.1
  226.1 8.7 %reduce-scatter.5.cloned.1.call-done = bf16[128,3696]{1,0:T(8,128)(2,1)} async-done(((bf16[2048,3696]{1,0:T(8,128)(2,1)}), bf16[128,3696]{1,0:T(8,128)(2,1)}) %reduce-scatter.5.cloned.1.call-update) | async-done | bytes 946192 | tf_op jit(solution)/shard_map/reduce_scatter | solution.py:97
  234.8 105.8 %reduce-scatter.3.cloned.1.call-done = bf16[128,3696]{1,0:T(8,128)(2,1)} async-done(((bf16[2048,3696]{1,0:T(8,128)(2,1)}), bf16[128,3696]{1,0:T(8,128)(2,1)}) %reduce-scatter.3.cloned.1.call-update) | async-done | bytes 946192 | tf_op jit(solution)/shard_map/reduce_scatter | solution.py:91
  340.7 2.0 fusion.8
  342.7 1.3 copy.14
  344.1 0.0 copy-done.1
  (3 shorter events, 0.0 us)
Async XLA Ops:
  6.5 46.7 %copy-start = (bf16[1,8192,128]{2,1,0:T(8,128)(2,1)S(1)}, bf16[1,8192,128]{2,1,0:T(8,128)(2,1)}, u32[]{:S(2)}) copy-start(bf16[1,8192,128]{2,1,0:T(8,128)(2,1)} %param.10) | copy-start | bytes 6291460
  6.5 1.5 copy-start.2
  6.5 66.7 %all-gather.2.cloned.1.call-start = ((), (), s32[]{:S(2)}) async-start(), calls=%async_computation.5 | async-start | bytes 2359296 | tf_op jit(solution)/shard_map/all_gather | solution.py:84
  8.0 13.3 %copy-start.3 = (bf16[256,512]{1,0:T(8,128)(2,1)S(1)}, bf16[256,512]{1,0:T(8,128)(2,1)}, u32[]{:S(2)}) copy-start(bf16[256,512]{1,0:T(8,128)(2,1)} %param.7) | copy-start | bytes 786436
  22.8 30.4 %all-to-all-start = ((bf16[128,8,512]{2,1,0:T(8,128)(2,1)}), bf16[128,8,512]{2,1,0:T(8,128)(2,1)S(1)}, u32[]{:S(2)}, u32[]{:S(2)}) async-start(bf16[128,8,512]{2,1,0:T(8,128)(2,1)} %fusion.9), calls=%async_computation | async-start | bytes 2097152 | tf_op jit(solution)/shard_map/all_to_all | solution.py:46
  59.0 50.4 %all-to-all-start.2 = ((bf16[8,64,3696]{2,1,0:T(8,128)(2,1)}), bf16[8,64,3696]{2,1,0:T(8,128)(2,1)}, u32[]{:S(2)}, u32[]{:S(2)}) async-start(bf16[8,64,3696]{2,1,0:T(8,128)(2,1)} %fusion.1), calls=%async_computation.3 | async-start | bytes 7602176 | tf_op jit(solution)/shard_map/all_to_all | solution.py:72
  64.6 170.2 %reduce-scatter.5.cloned.1.call-start = ((), (), s32[]{:S(2)}) async-start(), calls=%async_computation.7 | async-start | bytes 16154624 | tf_op jit(solution)/shard_map/reduce_scatter | solution.py:97
  149.1 5.4 %copy-start.4 = (bf16[2048,512]{1,0:T(8,128)(2,1)S(1)}, bf16[2048,512]{1,0:T(8,128)(2,1)}, u32[]{:S(2)}) copy-start(bf16[2048,512]{1,0:T(8,128)(2,1)} %all-gather.2.cloned.1.call-done) | copy-start | bytes 6291460
  149.1 50.2 %all-to-all-start.1 = ((bf16[8,64,3696]{2,1,0:T(8,128)(2,1)}), bf16[8,64,3696]{2,1,0:T(8,128)(2,1)}, u32[]{:S(2)}, u32[]{:S(2)}) async-start(bf16[8,64,3696]{2,1,0:T(8,128)(2,1)} %fusion), calls=%async_computation.1 | async-start | bytes 7602176 | tf_op jit(solution)/shard_map/all_to_all | solution.py:71
  154.6 186.1 %reduce-scatter.3.cloned.1.call-start = ((), (), s32[]{:S(2)}) async-start(), calls=%async_computation.6 | async-start | bytes 16154624 | tf_op jit(solution)/shard_map/reduce_scatter | solution.py:91
  226.1 117.9 %copy-start.1 = (bf16[1,8192,128]{2,1,0:T(8,128)(2,1)S(1)}, bf16[1,8192,128]{2,1,0:T(8,128)(2,1)}, u32[]{:S(2)}) copy-start(bf16[1,8192,128]{2,1,0:T(8,128)(2,1)} %param.10) | copy-start | bytes 6291460
Sparse Core Ops, SparseCore 0:
  9.1 28.7 all-gather.1
  136.4 98.3 reduce-scatter.4
  238.7 101.9 reduce-scatter.2
